TPU v7x, 512 devices: a whole 4x4x16 slice. The times are simulated.
512 devices in a mesh: dp: 8 (over z_hi, core), seq: 64 (over z_lo, y, x).
Axes of the slice: x: 4, y: 4, z: 16 (z_hi: 4, z_lo: 4; z = z_hi * 4 + z_lo), core: 2. Of those that a mesh axis runs over, the one named last changes fastest.
Arguments:
- query: bfloat16 [8, 8192, 512], P('dp', 'seq'), may hold values from -6 to 6
- key_in: bfloat16 [8, 8192, 128], P('dp', 'seq'), may hold values from -4.5 to 4.5
- value_in: bfloat16 [8, 8192, 128], P('dp', 'seq'), may hold values from -6 to 6
- out_gain: float32 [512], replicated, may hold values from 0.1 to 1.9
- cotangent: bfloat16 [8, 8192, 512], P('dp', 'seq'), may hold values from -6 to 6
Outputs:
- attended: bfloat16 [8, 8192, 512], P('dp', 'seq')
- grad_query: bfloat16 [8, 8192, 512], P('dp', 'seq')
- grad_key: bfloat16 [8, 8192, 128], P('dp', 'seq')
- grad_value: bfloat16 [8, 8192, 128], P('dp', 'seq')
- grad_gain: float32 [512], replicated
All inputs are finite; a program needn't handle non-finite values.
Results may differ from a plain program's by a relative error of at most 0.012.
The roundings to bfloat16 on the way count: a program that leaves them out, or rounds other values in their place, can miss the bound.
Values may be sent and summed in bfloat16 or wider, within the bound.
No kernel may reach another device: no remote copies, remote signals or barrier semaphores. Data moves between devices by JAX's collectives and lax.ppermute only.
A program may use at most 128 MiB of HBM per device.

v0:
```python
import math
import jax
import jax.numpy as jnp
from jax import lax
from jax.sharding import PartitionSpec as P

HEADS = 4
KEY = 128
VAL = 128


def to_rows(tokens, heads):
    positions = tokens.shape[0]
    width = tokens.shape[1] // heads
    return (
        tokens.reshape(positions, heads, width).transpose(1, 0, 2).reshape(heads * positions, width)
    )


def to_tokens(rows_in, heads):
    positions = rows_in.shape[0] // heads
    width = rows_in.shape[1]
    return (
        rows_in.reshape(heads, positions, width)
        .transpose(1, 0, 2)
        .reshape(positions, heads * width)
    )


def contract_first(left_mat, right_mat):
    return lax.dot_general(
        left_mat, right_mat, (((0,), (0,)), ((), ())), preferred_element_type=jnp.float32
    )


def contract_last(left_mat, right_mat):
    return lax.dot_general(
        left_mat, right_mat, (((1,), (1,)), ((), ())), preferred_element_type=jnp.float32
    )


def body(query, key_in, value_in, out_gain, cotangent):
    keys_all, values_all = (
        lax.all_gather(key_in, "seq", axis=1, tiled=True),
        lax.all_gather(value_in, "seq", axis=1, tiled=True),
    )
    key_mat = keys_all[0]
    value_mat = values_all[0]
    length = key_mat.shape[0]
    positions = query.shape[1]
    shards = lax.axis_size("seq")
    score_scale = 1.0 / math.sqrt(KEY)
    query_rows = to_rows(query[0], HEADS)
    scores = contract_last(query_rows, key_mat) * score_scale
    row_top = jnp.max(scores, axis=1, keepdims=True)
    expo_rows = jnp.exp(scores - row_top)
    weights = (expo_rows / jnp.sum(expo_rows, axis=1, keepdims=True)).astype(jnp.bfloat16)
    out_rows = jnp.dot(weights, value_mat, preferred_element_type=jnp.float32)
    out_tokens = to_tokens(out_rows, HEADS)
    attended = (out_tokens * out_gain).astype(jnp.bfloat16)
    upstream = cotangent[0].astype(jnp.float32)
    gain_total = lax.psum(jnp.sum(upstream * out_tokens, axis=0), ("dp", "seq"))
    token_total = lax.axis_size("dp") * shards * positions
    grad_gain = gain_total / math.sqrt(token_total)
    grad_out = (upstream * out_gain).astype(jnp.bfloat16)
    grad_rows = to_rows(grad_out, HEADS)
    delta_rows = jnp.sum(grad_rows.astype(jnp.float32) * out_rows, axis=1, keepdims=True)
    block_size = 2048
    block_starts = jnp.arange(length // block_size, dtype=jnp.int32) * block_size
    query_zero = jnp.zeros((query_rows.shape[0], KEY), jnp.float32)

    def score_grad(offset_at):
        key_part = lax.dynamic_slice_in_dim(key_mat, offset_at, block_size, 0)
        value_part = lax.dynamic_slice_in_dim(value_mat, offset_at, block_size, 0)
        weight_part = lax.dynamic_slice_in_dim(weights, offset_at, block_size, 1)
        d_prob = contract_last(grad_rows, value_part)
        d_score = (weight_part.astype(jnp.float32) * (d_prob - delta_rows)).astype(jnp.bfloat16)
        return (d_score, key_part, weight_part)

    def advance_both(query_acc, offset_at):
        d_score, key_part, weight_part = score_grad(offset_at)
        query_acc = query_acc + jnp.dot(d_score, key_part, preferred_element_type=jnp.float32)
        key_term = contract_first(d_score, query_rows) * score_scale
        value_term = contract_first(weight_part, grad_rows)
        return (query_acc, (key_term, value_term))

    query_acc, both_terms = lax.scan(advance_both, query_zero, block_starts)
    key_recv, value_recv = (
        lax.all_to_all(
            both_terms[0].reshape(shards, positions, KEY),
            "seq",
            split_axis=0,
            concat_axis=0,
            tiled=True,
        ),
        lax.all_to_all(
            both_terms[1].reshape(shards, positions, VAL),
            "seq",
            split_axis=0,
            concat_axis=0,
            tiled=True,
        ),
    )
    grad_key = jnp.sum(key_recv, axis=0)
    grad_value = jnp.sum(value_recv, axis=0)
    grad_query = to_tokens(query_acc * score_scale, HEADS).astype(jnp.bfloat16)
    return (
        attended[None],
        grad_query[None],
        grad_key.astype(jnp.bfloat16)[None],
        grad_value.astype(jnp.bfloat16)[None],
        grad_gain,
    )


def solution(mesh):
    placed = (
        P("dp", "seq", None),
        P("dp", "seq", None),
        P("dp", "seq", None),
        P(),
        P("dp", "seq", None),
    )
    return jax.shard_map(
        body,
        mesh=mesh,
        in_specs=placed,
        out_specs=(
            P("dp", "seq", None),
            P("dp", "seq", None),
            P("dp", "seq", None),
            P("dp", "seq", None),
            P(),
        ),
        check_vma=False,
    )
```

profile of v0, /device:TPU:1, one launch (start us, length us, event | category | flops | bytes accessed | tf_op | source)
XLA Modules:
  0.0 1053.3 jit_solution(2763086969932441278)
XLA Ops:
  7.2 0.0 all-gather.3.cloned.1.call-start
  7.2 0.7 all-gather.3.cloned.1.call-update
  7.9 0.0 all-gather.5.cloned.1.call-start
  7.9 0.7 all-gather.5.cloned.1.call-update
  8.7 1.0 reshape.111
  9.7 0.9 reshape_squeeze.3
  10.7 312.2 %all-gather.3.cloned.1.call-done = bf16[1,8192,128]{2,1,0:T(8,128)(2,1)} async-done(((bf16[1,128,128]{2,1,0:T(8,128)(2,1)}), bf16[1,8192,128]{2,1,0:T(8,128)(2,1)}) %all-gather.3.cloned.1.call-update) | async-done | bytes 2097168 | tf_op jit(solution)/shard_map/all_gather | solution.py:44
  322.9 9.6 multiply_reduce_fusion
  332.5 8.6 fusion.8
  341.1 0.0 copy-start
  341.1 10.3 divide_convert_fusion
  351.5 326.2 %all-gather.5.cloned.1.call-done = bf16[1,8192,128]{2,1,0:T(8,128)(2,1)} async-done(((bf16[1,128,128]{2,1,0:T(8,128)(2,1)}), bf16[1,8192,128]{2,1,0:T(8,128)(2,1)}) %all-gather.5.cloned.1.call-update) | async-done | bytes 2097168 | tf_op jit(solution)/shard_map/all_gather | solution.py:45
  677.7 0.0 copy-done
  677.7 6.3 multiply_reduce_fusion.1
  684.0 0.2 multiply_reduce_fusion.2
  684.2 77.3 %while.15 = (s32[]{:T(128)}, f32[512,128]{1,0:T(8,128)S(1)}, f32[4,2048,128]{2,1,0:T(8,128)}, f32[4,2048,128]{2,1,0:T(8,128)}, s32[4]{0:T(128)S(1)}, /*index=5*/...) while((s32[]{:T(128)}, f32[512,128]{1,0:T(8,128)S(1)}, ...), condition=%wide.region_4.0_spmd.clone, body=%wide.region_3.0_spmd.clone.sunk | while | flops 1078329344 | bytes 22939864 | solution.py:87
  684.2 0.6 dynamic_slice.29
  686.7 2.9 constant_dynamic-slice_fusion.2
  689.6 2.5 copy.22
  692.1 3.9 fusion.40
  696.0 2.4 convolution_add_fusion.2
  698.5 3.4 fusion.41
  701.8 1.8 fusion.42
  703.6 0.6 dynamic_slice.29
  706.2 2.9 constant_dynamic-slice_fusion.2
  709.1 2.5 copy.22
  711.6 3.9 fusion.40
  715.5 2.5 convolution_add_fusion.2
  717.9 3.3 fusion.41
  721.2 1.7 fusion.42
  722.9 0.6 dynamic_slice.29
  725.4 2.9 constant_dynamic-slice_fusion.2
  728.3 2.5 copy.22
  730.9 3.9 fusion.40
  734.8 2.5 convolution_add_fusion.2
  737.2 3.3 fusion.41
  740.5 1.7 fusion.42
  742.2 0.6 dynamic_slice.29
  744.7 2.9 constant_dynamic-slice_fusion.2
  747.6 2.5 copy.22
  750.1 3.9 fusion.40
  754.0 2.5 convolution_add_fusion.2
  756.5 3.3 fusion.41
  759.7 1.7 fusion.42
  761.5 60.0 %all_to_all.10 = f32[64,128,128]{2,1,0:T(8,128)} all-to-all(f32[64,128,128]{2,1,0:T(8,128)} %bitcast.85), channel_id=1, replica_groups=mesh['dp'=8,'seq'=64] {'seq'}, dimensions={0} | all-to-all | bytes 8388608 | tf_op jit(solution)/shard_map/all_to_all | solution.py:89
  821.4 5.7 all-to-all-start.1
  827.1 0.2 copy.11
  827.3 0.1 reshape.107
  827.4 0.1 copy.20
  827.5 0.7 convert_element_type.88
  828.3 210.9 %psum.7 = f32[512]{0:T(512)S(1)} all-reduce(f32[512]{0:T(512)S(1)} %bitcast.95), channel_id=1, replica_groups=mesh['dp'=8,'seq'=64] {'dp','seq'}, use_global_device_ids=true, to_apply=%region_8.9 | all-reduce | flops 512 | bytes 4096 | tf_op jit(solution)/shard_map/psum | solution.py:62
  1039.2 0.6 broadcast_multiply_fusion
  1039.8 0.7 multiply_convert_fusion.2
  1040.4 3.0 reduce_sum.49
  1043.5 0.0 all-to-all-done.1
  1043.5 3.0 reduce_sum.50
  (6 shorter events, 0.1 us)
Async XLA Ops:
  7.2 315.7 %all-gather.3.cloned.1.call-start = ((), (), s32[]{:S(2)}) async-start(), calls=%async_computation.2 | async-start | bytes 2129920 | tf_op jit(solution)/shard_map/all_gather | solution.py:44
  7.9 669.8 %all-gather.5.cloned.1.call-start = ((), (), s32[]{:S(2)}) async-start(), calls=%async_computation.3 | async-start | bytes 2129920 | tf_op jit(solution)/shard_map/all_gather | solution.py:45
  341.1 336.5 %copy-start = (f32[512]{0:T(512)S(1)}, f32[512]{0:T(512)}, u32[]{:S(2)}) copy-start(f32[512]{0:T(512)} %param.10) | copy-start | bytes 6148
  821.4 222.0 %all-to-all-start.1 = ((f32[64,128,128]{2,1,0:T(8,128)}), f32[64,128,128]{2,1,0:T(8,128)}, u32[]{:S(2)}, u32[]{:S(2)}) async-start(f32[64,128,128]{2,1,0:T(8,128)} %bitcast.86), calls=%async_computation.1 | async-start | bytes 8388608 | tf_op jit(solution)/shard_map/all_to_all | solution.py:96
Sparse Core Ops, SparseCore 0:
  10.1 312.7 all-gather.2
  324.9 352.6 all-gather.4
where the time goes:
time: 1050 us
  waiting for transfers between devices  640 us (61%)
  blocking collectives  271 us (26%)
  matrix products  61.4 us (6%)
  local copies, waits for them, and re-layouts  27.1 us (3%)
  other arithmetic  26.4 us (3%)
  between operations  14.1 us (1%)
    all_gather x1, waiting for transfers between devices, body(): lax.all_gather(value_in, 'seq', axis=1, tiled=True)  326 us
    all_gather x1, waiting for transfers between devices, body(): lax.all_gather(key_in, 'seq', axis=1, tiled=True)  312 us
    psum x1, blocking collectives, body(): gain_total = lax.psum(jnp.sum(upstream * out_tokens, axis=0), ('dp', 'seq'))  211 us
    all_to_all x1, blocking collectives, body(): lax.all_to_all(both_terms[0].reshape(shards, positions, KEY), 'seq', spli...  60 us
    dot_general x5, matrix products, contract_last(): lax.dot_general(left_mat, right_mat, (((1,), (1,)), ((), ())), preferred_...  25.2 us
    dynamic_slice x8, local copies, waits for them, and re-layouts, score_grad(): weight_part = lax.dynamic_slice_in_dim(weights, offset_at, block_size, 1)  21.7 us
  transfers between devices with their start and end apart: 3, of which 2 were waited for; matrix products, arithmetic and copies ran while one was open for 3% of the time, Pallas kernels for 0%

commit v1 on v0

--- a/solution.py
+++ b/solution.py
@@ -1,12 +1,27 @@
+import functools
 import math
 import jax
 import jax.numpy as jnp
 from jax import lax
 from jax.sharding import PartitionSpec as P
+from jax.lax import all_to_all, psum
 
 HEADS = 4
 KEY = 128
 VAL = 128
+
+
+def _lift_spot(content, shard_axis):
+    found_now = jnp.concatenate(
+        all_to_all(
+            jnp.stack(psum(1, shard_axis) * [content], 0), shard_axis, split_axis=0, concat_axis=0
+        ),
+        1,
+    )
+    return found_now
+
+
+match_the_lines = functools.partial(_lift_spot, shard_axis="seq")
 
 
 def to_rows(tokens, heads):
@@ -41,7 +56,7 @@
 
 def body(query, key_in, value_in, out_gain, cotangent):
     keys_all, values_all = (
-        lax.all_gather(key_in, "seq", axis=1, tiled=True),
+        match_the_lines(key_in),
         lax.all_gather(value_in, "seq", axis=1, tiled=True),
     )
     key_mat = keys_all[0]

time: 1050 us -> 713 us (0.68)
  waiting for transfers between devices: 640 us -> 284 us
  starting transfers between devices: 5.74 us -> 18.5 us
    all_gather x1 -> x0, waiting for transfers between devices: 312 us -> none  [body(): lax.all_gather(key_in, 'seq', axis=1, tiled=True)]
    all_gather x1, waiting for transfers between devices: 326 us -> 235 us  [body(): lax.all_gather(value_in, 'seq', axis=1, tiled=True)]
    all_to_all x0 -> x1, waiting for transfers between devices: none -> 48 us  [_lift_spot(): all_to_all(jnp.stack(psum(1, shard_axis) * [content], 0), shard_axis, spl...]
    all_to_all x0 -> x1, starting transfers between devices: none -> 12.8 us  [_lift_spot(): all_to_all(jnp.stack(psum(1, shard_axis) * [content], 0), shard_axis, spl...]
  transfers between devices with their start and end apart: 3 -> 3, of which waited for: 2 -> 2; matrix products, arithmetic and copies ran while one was open for 3% -> 5% of each run, Pallas kernels for 0% -> 0%
where the time goes in v1:
time: 713 us; the launch traced here: 712 us
  waiting for transfers between devices  284 us (40%)
  blocking collectives  271 us (38%)
  matrix products  61.4 us (9%)
  local copies, waits for them, and re-layouts  27.9 us (4%)
  other arithmetic  26.5 us (4%)
  starting transfers between devices  18.5 us (3%)
  between operations  14.2 us (2%)
  loops' own time  7.85 us (1%)
    all_gather x1, waiting for transfers between devices, body(): lax.all_gather(value_in, 'seq', axis=1, tiled=True)  235 us
    psum x1, blocking collectives, body(): gain_total = lax.psum(jnp.sum(upstream * out_tokens, axis=0), ('dp', 'seq'))  211 us
    all_to_all x1, blocking collectives, body(): lax.all_to_all(both_terms[0].reshape(shards, positions, KEY), 'seq', spli...  60 us
    all_to_all x1, waiting for transfers between devices, _lift_spot(): all_to_all(jnp.stack(psum(1, shard_axis) * [content], 0), shard_axis, spl...  48 us
    dot_general x5, matrix products, contract_last(): lax.dot_general(left_mat, right_mat, (((1,), (1,)), ((), ())), preferred_...  25.2 us
    dynamic_slice x8, local copies, waits for them, and re-layouts, score_grad(): weight_part = lax.dynamic_slice_in_dim(weights, offset_at, block_size, 1)  21.7 us
    dot_general x8, matrix products, contract_first(): lax.dot_general(left_mat, right_mat, (((0,), (0,)), ((), ())), preferred_...  20.1 us
  transfers between devices with their start and end apart: 3, of which 2 were waited for; matrix products, arithmetic and copies ran while one was open for 5% of the time, Pallas kernels for 0%

profile of v1, /device:TPU:1, one launch (start us, length us, event | category | flops | bytes accessed | tf_op | source)
XLA Modules:
  0.0 711.5 jit_solution(8558143715272585328)
XLA Ops:
  7.2 0.0 copy-start
  7.2 0.0 copy-start.1
  7.2 2.7 stack.2
  9.8 12.8 %all-to-all-start = ((bf16[64,1,128,128]{3,2,1,0:T(8,128)(2,1)}), bf16[64,1,128,128]{3,2,1,0:T(8,128)(2,1)}, u32[]{:S(2)}, u32[]{:S(2)}) async-start(bf16[64,1,128,128]{3,2,1,0:T(8,128)(2,1)} %stack.2), calls=%async_computation | async-start | bytes 4194304 | tf_op jit(solution)/shard_map/all_to_all | solution.py:16
  22.7 0.0 all-gather.2.cloned.1.call-start
  22.7 0.7 all-gather.2.cloned.1.call-update
  23.4 0.0 copy-done
  23.4 0.1 reshape.114
  23.5 0.0 copy-done.1
  23.6 48.0 %all-to-all-done = bf16[64,1,128,128]{3,2,1,0:T(8,128)(2,1)} async-done(((bf16[64,1,128,128]{3,2,1,0:T(8,128)(2,1)}), bf16[64,1,128,128]{3,2,1,0:T(8,128)(2,1)}, u32[]{:S(2)}, u32[]{:S(2)}) %all-to-all-start) | async-done | bytes 2097184 | tf_op jit(solution)/shard_map/all_to_all | solution.py:16
  71.6 9.6 %multiply_reduce_fusion = (f32[512]{0:T(512)S(1)}, f32[512,8192]{1,0:T(8,128)}) fusion(bf16[512,128]{1,0:T(8,128)(2,1)S(1)} %bitcast.80, bf16[8192,128]{1,0:T(8,128)(2,1)} %bitcast.3), kind=kOutput, calls=%fused_computation.15 | convolution fusion | flops 1082129920 | bytes 19007488 | tf_op jit(solution)/shard_map/dot_general | solution.py:52
  81.3 8.6 %fusion.8 = f32[512]{0:T(512)S(1)} fusion(f32[512,8192]{1,0:T(8,128)} %get-tuple-element.150, f32[512]{0:T(512)S(1)} %get-tuple-element.149), kind=kLoop, calls=%fused_computation.16 | loop fusion | flops 12582400 | bytes 16781312 | tf_op jit(solution)/shard_map/reduce_sum | solution.py:72
  89.9 0.0 copy-start.2
  89.9 10.3 %divide_convert_fusion = bf16[512,8192]{1,0:T(8,128)(2,1)} fusion(f32[512,8192]{1,0:T(8,128)} %get-tuple-element.150, f32[512]{0:T(512)S(1)} %fusion.8, f32[512]{0:T(512)S(1)} %get-tuple-element.149), kind=kLoop, calls=%fused_computation.13 | loop fusion | flops 16777216 | bytes 25169920 | tf_op jit(solution)/shard_map/convert_element_type | solution.py:72
  100.2 235.4 %all-gather.2.cloned.1.call-done = bf16[1,8192,128]{2,1,0:T(8,128)(2,1)} async-done(((bf16[1,128,128]{2,1,0:T(8,128)(2,1)}), bf16[1,8192,128]{2,1,0:T(8,128)(2,1)}) %all-gather.2.cloned.1.call-update) | async-done | bytes 2097168 | tf_op jit(solution)/shard_map/all_gather | solution.py:60
  335.6 0.0 copy-done.2
  335.6 6.3 multiply_reduce_fusion.1
  342.0 0.2 multiply_reduce_fusion.2
  342.1 77.3 %while.15 = (s32[]{:T(128)}, f32[512,128]{1,0:T(8,128)S(1)}, f32[4,2048,128]{2,1,0:T(8,128)}, f32[4,2048,128]{2,1,0:T(8,128)}, s32[4]{0:T(128)S(1)}, /*index=5*/...) while((s32[]{:T(128)}, f32[512,128]{1,0:T(8,128)S(1)}, ...), condition=%wide.region_4.0_spmd.clone, body=%wide.region_3.0_spmd.clone.sunk | while | flops 1078329344 | bytes 22939864 | solution.py:102
  342.1 0.6 dynamic_slice.29
  344.7 2.9 constant_dynamic-slice_fusion.2
  347.6 2.5 copy.28
  350.1 3.9 fusion.39
  354.0 2.5 convolution_add_fusion.2
  356.5 3.4 fusion.40
  359.8 1.8 fusion.41
  361.6 0.6 dynamic_slice.29
  364.1 2.9 constant_dynamic-slice_fusion.2
  367.0 2.5 copy.28
  369.6 3.9 fusion.39
  373.5 2.4 convolution_add_fusion.2
  375.9 3.3 fusion.40
  379.2 1.7 fusion.41
  380.9 0.6 dynamic_slice.29
  383.4 2.9 constant_dynamic-slice_fusion.2
  386.3 2.5 copy.28
  388.9 3.9 fusion.39
  392.7 2.4 convolution_add_fusion.2
  395.2 3.3 fusion.40
  398.5 1.7 fusion.41
  400.2 0.6 dynamic_slice.29
  402.7 2.9 constant_dynamic-slice_fusion.2
  405.6 2.5 copy.28
  408.1 3.9 fusion.39
  412.0 2.5 convolution_add_fusion.2
  414.5 3.3 fusion.40
  417.7 1.7 fusion.41
  419.5 60.0 %all_to_all.15 = f32[64,128,128]{2,1,0:T(8,128)} all-to-all(f32[64,128,128]{2,1,0:T(8,128)} %bitcast.82), channel_id=1, replica_groups=mesh['dp'=8,'seq'=64] {'seq'}, dimensions={0} | all-to-all | bytes 8388608 | tf_op jit(solution)/shard_map/all_to_all | solution.py:104
  479.5 5.7 all-to-all-start.2
  485.1 0.2 copy.17
  485.3 0.1 reshape.110
  485.5 0.1 copy.26
  485.6 0.7 convert_element_type.88
  486.3 211.1 %psum.7 = f32[512]{0:T(512)S(1)} all-reduce(f32[512]{0:T(512)S(1)} %bitcast.93), channel_id=1, replica_groups=mesh['dp'=8,'seq'=64] {'dp','seq'}, use_global_device_ids=true, to_apply=%region_8.9 | all-reduce | flops 512 | bytes 4096 | tf_op jit(solution)/shard_map/psum | solution.py:77
  697.3 0.6 broadcast_multiply_fusion
  697.9 0.7 multiply_convert_fusion.2
  698.6 3.0 reduce_sum.49
  701.6 0.0 all-to-all-done.2
  701.6 3.0 reduce_sum.50
  (7 shorter events, 0.1 us)
Async XLA Ops:
  7.2 16.3 %copy-start = (bf16[1,128,512]{2,1,0:T(8,128)(2,1)S(1)}, bf16[1,128,512]{2,1,0:T(8,128)(2,1)}, u32[]{:S(2)}) copy-start(bf16[1,128,512]{2,1,0:T(8,128)(2,1)} %param.11) | copy-start | bytes 393220
  7.2 16.3 %copy-start.1 = (bf16[1,128,512]{2,1,0:T(8,128)(2,1)S(1)}, bf16[1,128,512]{2,1,0:T(8,128)(2,1)}, u32[]{:S(2)}) copy-start(bf16[1,128,512]{2,1,0:T(8,128)(2,1)} %param.7) | copy-start | bytes 393220
  9.8 61.8 %all-to-all-start = ((bf16[64,1,128,128]{3,2,1,0:T(8,128)(2,1)}), bf16[64,1,128,128]{3,2,1,0:T(8,128)(2,1)}, u32[]{:S(2)}, u32[]{:S(2)}) async-start(bf16[64,1,128,128]{3,2,1,0:T(8,128)(2,1)} %stack.2), calls=%async_computation | async-start | bytes 4194304 | tf_op jit(solution)/shard_map/all_to_all | solution.py:16
  22.7 313.0 %all-gather.2.cloned.1.call-start = ((), (), s32[]{:S(2)}) async-start(), calls=%async_computation.3 | async-start | bytes 2129920 | tf_op jit(solution)/shard_map/all_gather | solution.py:60
  89.9 245.8 %copy-start.2 = (f32[512]{0:T(512)S(1)}, f32[512]{0:T(512)}, u32[]{:S(2)}) copy-start(f32[512]{0:T(512)} %param.10) | copy-start | bytes 6148
  479.5 222.2 %all-to-all-start.2 = ((f32[64,128,128]{2,1,0:T(8,128)}), f32[64,128,128]{2,1,0:T(8,128)}, u32[]{:S(2)}, u32[]{:S(2)}) async-start(f32[64,128,128]{2,1,0:T(8,128)} %bitcast.83), calls=%async_computation.2 | async-start | bytes 8388608 | tf_op jit(solution)/shard_map/all_to_all | solution.py:111
Sparse Core Ops, SparseCore 0:
  25.5 310.0 all-gather.1
